TPU v7x, 256 devices: a whole 4x4x8 slice. The times are simulated.
256 devices in a mesh: seq: 64 (over z, y, core), head: 4 (over x).
Axes of the slice: x: 4, y: 4, z: 8, core: 2. Of those that a mesh axis runs over, the one named last changes fastest.
Arguments:
- query: bfloat16 [40960, 2048], P(('seq', 'head')), may hold values from -5 to 5
- key: bfloat16 [40960, 2048], P(('seq', 'head')), may hold values from -5 to 5
- value: bfloat16 [40960, 2048], P(('seq', 'head')), may hold values from -6 to 6
- grad_out: bfloat16 [40960, 2048], P(('seq', 'head')), may hold values from -6 to 6
- rand_blocks: int32 [640, 3], replicated, may hold values from 0 to 639, as said below
Outputs:
- grad_query: bfloat16 [40960, 2048], P(('seq', 'head'))
- grad_key: bfloat16 [40960, 2048], P(('seq', 'head'))
- grad_value: bfloat16 [40960, 2048], P(('seq', 'head'))
Inputs may be any that keep to these rules, and one draw needn't show every extreme that they name: `rand_blocks`: row j lists the 3 random key blocks of query block j. Block b lies on index b // 10 of seq. The blocks of one row lie on 3 different indices. No listed block lies on index 0 or on the index of the query block itself. The query blocks of one index of seq list at most 1 block lying on any one other index.
All inputs are finite; a program needn't handle non-finite values.
Results may differ from a plain program's by a relative error of at most 0.008.
Values may be sent and summed in bfloat16 or wider, within the bound.
No kernel may reach another device: no remote copies, remote signals or barrier semaphores. Data moves between devices by JAX's collectives and lax.ppermute only.
A program may use at most 384 MiB of HBM per device.

v0:
```python
import jax
import jax.numpy as jnp
from jax import lax
from jax.sharding import PartitionSpec as P

HD = 128
BLOCK = 64
G = 2
R = 3
big_negative = -1e30


def broadcast(block, axis, source):
    peers = lax.axis_size(axis)
    block = jnp.where(lax.axis_index(axis) == source, block, jnp.zeros_like(block))
    inner = 8 if peers % 8 == 0 else 1
    if inner > 1 and source == 0:
        outer = peers // inner
        received = [lax.ppermute(block, axis, [(0, k * inner)]) for k in range(1, outer)]
        for part in received:
            block = block + part
        received = [
            lax.ppermute(block, axis, [(z * inner, z * inner + k) for z in range(outer)])
            for k in range(1, inner)
        ]
        for part in received:
            block = block + part
        return block
    step = 1
    while step * 2 < peers:
        step *= 2
    while step >= 1:
        pairs = [(i, i + step) for i in range(0, peers, 2 * step) if i + step < peers]
        block = block + lax.ppermute(block, axis, pairs)
        step //= 2
    return block


def reduce_to_first(block, axis):
    peers = lax.axis_size(axis)
    step = 1
    while step < peers:
        radix = 4 if peers % (step * 4) == 0 else 2
        received = [
            lax.ppermute(block, axis, [(i + k * step, i) for i in range(0, peers, radix * step)])
            for k in range(1, radix)
        ]
        for part in received:
            block = block + part
        step *= radix
    return block


def extended_2(shard, sides, width):
    for axis, dim in sides:
        peers, length = (lax.axis_size(axis), shard.shape[dim])
        up = [(i, (i + 1) % peers) for i in range(peers - 1)]
        down = [(j, i) for i, j in up]
        last = lax.slice_in_dim(shard, length - width, length, axis=dim)
        leading = lax.slice_in_dim(shard, 0, width, axis=dim)
        before = lax.ppermute(last, axis, up)
        after = lax.ppermute(leading, axis, down)
        shard = jnp.concatenate([before, shard, after], axis=dim)
    return shard


def request_plan(requested, device, per_dev):
    wanted_row = requested[device]
    owners = wanted_row // per_dev
    within = wanted_row % per_dev
    usable = jnp.ones(wanted_row.shape, jnp.bool_)
    positions = jnp.arange(owners.shape[0])
    earlier = (owners[:, None] == owners[None, :]) & (positions[None, :] < positions[:, None])
    slot_rank = jnp.sum(earlier.astype(jnp.int32), axis=1)
    return (owners, within, slot_rank, usable)


def local_chunk(queries, out_grads, own_pairs, global_pairs, extended, device, seq_count):
    tokens, features = queries.shape
    head_count = features // HD
    per_dev = tokens // BLOCK
    score_scale = HD ** (-0.5)
    left_pair = extended[:, :BLOCK]
    right_pair = extended[:, -BLOCK:]
    framed = jnp.concatenate([left_pair[:, None], own_pairs, right_pair[:, None]], axis=1)
    window = jnp.stack(
        [framed[:, 0:per_dev], framed[:, 1 : per_dev + 1], framed[:, 2 : per_dev + 2]], axis=2
    )
    global_slots = jnp.broadcast_to(global_pairs[:, None], (2, per_dev, G, BLOCK, features))
    local = jnp.concatenate([window, global_slots], axis=2)
    local_count = 3 + G
    local_keys = local[0].reshape(per_dev, local_count, BLOCK, head_count, HD)
    local_values = local[1].reshape(per_dev, local_count, BLOCK, head_count, HD)
    block_index = device * per_dev + jnp.arange(per_dev)
    glob_index = jnp.arange(G)
    intersections = jnp.abs(glob_index[None, :] - block_index[:, None]) <= 1
    live_local = jnp.concatenate(
        [
            (block_index >= 1)[:, None],
            jnp.ones((per_dev, 1), jnp.bool_),
            (block_index <= seq_count * per_dev - 2)[:, None],
            jnp.logical_not(intersections),
        ],
        axis=1,
    )
    query_blocks = queries.reshape(per_dev, BLOCK, head_count, HD)
    dout_blocks = out_grads.reshape(per_dev, BLOCK, head_count, HD)
    scores_local = (
        jnp.einsum(
            "bxhd,bkyhd->bhxky", query_blocks, local_keys, preferred_element_type=jnp.float32
        )
        * score_scale
    )
    scores_local = jnp.where(live_local[:, None, None, :, None], scores_local, big_negative)
    grads_local = jnp.einsum(
        "bxhd,bkyhd->bhxky", dout_blocks, local_values, preferred_element_type=jnp.float32
    )
    max_local = jnp.max(scores_local, axis=(3, 4), keepdims=True)
    return (
        local_keys,
        local_values,
        query_blocks,
        dout_blocks,
        scores_local,
        grads_local,
        max_local,
    )


def attend_chunk(
    queries, outgoing, state, chooser, my_slot, my_usable, device, seq_count, capacity, hold=()
):
    tokens, features = queries.shape
    head_count = features // HD
    per_dev = tokens // BLOCK
    rand_count = per_dev * R
    score_scale = HD ** (-0.5)
    local_keys, local_values, query_blocks, dout_blocks, scores_local, grads_local, max_local = (
        state
    )
    incoming = lax.all_to_all(outgoing, "seq", split_axis=0, concat_axis=0, tiled=True)
    if hold:
        incoming, hold = lax.optimization_barrier((incoming, hold))
    fetched = incoming[my_slot]
    randoms = fetched.reshape(per_dev, R, 2, BLOCK, features)
    rand_keys = randoms[:, :, 0].reshape(per_dev, R, BLOCK, head_count, HD)
    rand_values = randoms[:, :, 1].reshape(per_dev, R, BLOCK, head_count, HD)
    scores_rand = (
        jnp.einsum("bxhd,bkyhd->bhxky", query_blocks, rand_keys, preferred_element_type=jnp.float32)
        * score_scale
    )
    grads_rand = jnp.einsum(
        "bxhd,bkyhd->bhxky", dout_blocks, rand_values, preferred_element_type=jnp.float32
    )
    row_max = jnp.maximum(max_local, jnp.max(scores_rand, axis=(3, 4), keepdims=True))
    weights_local = jnp.exp(scores_local - row_max)
    weights_rand = jnp.exp(scores_rand - row_max)
    row_total = jnp.sum(weights_local, axis=(3, 4), keepdims=True) + jnp.sum(
        weights_rand, axis=(3, 4), keepdims=True
    )
    probs_local = weights_local / row_total
    probs_rand = weights_rand / row_total
    row_dot = jnp.sum(probs_local * grads_local, axis=(3, 4), keepdims=True) + jnp.sum(
        probs_rand * grads_rand, axis=(3, 4), keepdims=True
    )
    dscores_rand = (probs_rand * (grads_rand - row_dot)).astype(jnp.bfloat16)
    low_rand = probs_rand.astype(jnp.bfloat16)
    key_rand = (
        jnp.einsum(
            "bhxky,bxhd->bkyhd", dscores_rand, query_blocks, preferred_element_type=jnp.float32
        )
        * score_scale
    )
    value_rand = jnp.einsum(
        "bhxky,bxhd->bkyhd", low_rand, dout_blocks, preferred_element_type=jnp.float32
    )
    rand_terms = (
        jnp.stack([key_rand, value_rand])
        .reshape(2, rand_count, BLOCK, features)
        .transpose(1, 0, 2, 3)
        .astype(jnp.bfloat16)
    )
    dscores_local = (probs_local * (grads_local - row_dot)).astype(jnp.bfloat16)
    low_local = probs_local.astype(jnp.bfloat16)
    key_global = (
        jnp.einsum(
            "bhxky,bxhd->kyhd",
            dscores_local[:, :, :, 3:],
            query_blocks,
            preferred_element_type=jnp.float32,
        )
        * score_scale
    )
    value_global = jnp.einsum(
        "bhxky,bxhd->kyhd", low_local[:, :, :, 3:], dout_blocks, preferred_element_type=jnp.float32
    )
    halves = jnp.stack([key_global, value_global]).reshape(2, G, BLOCK, features)
    is_even = device % 2 == 0
    partner = [(i, i ^ 1) for i in range(seq_count)]
    handed = lax.ppermute(jnp.where(is_even, halves[1], halves[0]), "seq", partner)
    kept = jnp.where(is_even, halves[0], halves[1]) + handed
    target = jnp.where(my_usable, my_slot, seq_count * capacity)
    placer = (target[:, None] == jnp.arange(seq_count * capacity)[None, :]).astype(jnp.bfloat16)
    outgoing_back = jnp.einsum(
        "js,jkxf->skxf", placer, rand_terms, preferred_element_type=jnp.float32
    ).astype(jnp.bfloat16)
    outgoing_back = jnp.concatenate([kept[None].astype(jnp.bfloat16), outgoing_back[1:]], axis=0)
    arrived = lax.all_to_all(outgoing_back, "seq", split_axis=0, concat_axis=0, tiled=True)
    firsts = arrived.reshape(seq_count, capacity, 2, BLOCK, features)[:, 0]
    firsts = firsts.reshape(seq_count // 2, 2, G, BLOCK, features)
    everywhere = jnp.sum(firsts.astype(jnp.float32), axis=0)
    query_grads = (
        jnp.einsum(
            "bhxky,bkyhd->bxhd", dscores_local, local_keys, preferred_element_type=jnp.float32
        )
        + jnp.einsum(
            "bhxky,bkyhd->bxhd", dscores_rand, rand_keys, preferred_element_type=jnp.float32
        )
    ) * score_scale
    key_terms = (
        jnp.einsum(
            "bhxky,bxhd->bkyhd",
            dscores_local[:, :, :, :3],
            query_blocks,
            preferred_element_type=jnp.float32,
        )
        * score_scale
    )
    value_terms = jnp.einsum(
        "bhxky,bxhd->bkyhd", low_local[:, :, :, :3], dout_blocks, preferred_element_type=jnp.float32
    )
    pair_terms = jnp.stack([key_terms, value_terms]).reshape(2, per_dev, 3, BLOCK, features)
    framed_sum = jnp.pad(pair_terms[:, :, 0], ((0, 0), (0, 2), (0, 0), (0, 0)))
    framed_sum = framed_sum + jnp.pad(pair_terms[:, :, 1], ((0, 0), (1, 1), (0, 0), (0, 0)))
    framed_sum = framed_sum + jnp.pad(pair_terms[:, :, 2], ((0, 0), (2, 0), (0, 0), (0, 0)))
    totals = framed_sum[:, 1 : per_dev + 1]
    rim_terms = jnp.concatenate([framed_sum[:, 0], framed_sum[:, -1]], axis=1)
    padded_global = jnp.pad(everywhere, ((0, 0), (0, per_dev - G), (0, 0), (0, 0))) * (
        device == 0
    ).astype(jnp.float32)
    totals = totals + padded_global
    collected = jnp.einsum(
        "dcb,dcsxf->sbxf",
        chooser.astype(jnp.bfloat16),
        arrived.reshape(seq_count, capacity, 2, BLOCK, features),
        preferred_element_type=jnp.float32,
    )
    totals = totals + collected
    return (query_grads.reshape(tokens, features), totals, rim_terms, hold)


def on_device(query, key, value, grad_out, rand_blocks):
    kv_stacked = jnp.stack([key, value])
    kv_stacked = lax.all_to_all(kv_stacked, "head", split_axis=2, concat_axis=1, tiled=True)
    keys, values = (kv_stacked[0], kv_stacked[1])
    qo_stacked = jnp.stack([query, grad_out])
    qo_stacked = lax.all_to_all(qo_stacked, "head", split_axis=2, concat_axis=1, tiled=True)
    queries, out_grads = (qo_stacked[0], qo_stacked[1])
    tokens, features = queries.shape
    head_count = features // HD
    per_dev = tokens // BLOCK
    seq_count = lax.axis_size("seq")
    device = lax.axis_index("seq")
    capacity = (per_dev * R + seq_count - 3) // (seq_count - 2)
    rand_count = per_dev * R
    score_scale = HD ** (-0.5)
    requested = rand_blocks.reshape(seq_count, rand_count)
    owners_all, within_all, rank_all, usable_all = jax.vmap(
        lambda sender: request_plan(requested, sender, per_dev)
    )(jnp.arange(seq_count, dtype=jnp.int32))
    to_me = usable_all & (owners_all == device)
    slot_ids = jnp.arange(capacity)
    block_ids = jnp.arange(per_dev)
    matches = (
        to_me[:, :, None, None]
        & (rank_all[:, :, None, None] == slot_ids[None, None, :, None])
        & (within_all[:, :, None, None] == block_ids[None, None, None, :])
    )
    chooser = jnp.sum(matches.astype(jnp.float32), axis=1)
    my_owners, my_within, my_rank, my_usable = request_plan(requested, device, per_dev)
    my_slot = jnp.clip(my_owners, 0, seq_count - 1) * capacity + my_rank
    own_pairs = jnp.stack([keys, values]).reshape(2, per_dev, BLOCK, features)
    served = jnp.einsum(
        "dcb,sbxf->dcsxf",
        chooser.astype(jnp.bfloat16),
        own_pairs,
        preferred_element_type=jnp.float32,
    ).astype(jnp.bfloat16)
    outgoing = served.reshape(seq_count * capacity, 2, BLOCK, features)
    leading = jnp.stack([keys[: G * BLOCK], values[: G * BLOCK]])
    global_pairs = broadcast(leading, "seq", 0).reshape(2, G, BLOCK, features)
    extended = extended_2(jnp.stack([keys, values]), (("seq", 1),), BLOCK)
    outgoing, global_pairs, extended = lax.optimization_barrier((outgoing, global_pairs, extended))
    chunk_heads = 2 if head_count % 2 == 0 else 1
    chunk_width = chunk_heads * HD
    states = [
        local_chunk(
            queries[:, c0 : c0 + chunk_width],
            out_grads[:, c0 : c0 + chunk_width],
            own_pairs[..., c0 : c0 + chunk_width],
            global_pairs[..., c0 : c0 + chunk_width],
            extended[..., c0 : c0 + chunk_width],
            device,
            seq_count,
        )
        for c0 in range(0, features, chunk_width)
    ]
    pieces = []
    held = ()
    for index, c0 in enumerate(range(0, features, chunk_width)):
        state = states[index] if index == 0 else held[index - 1]
        piece = attend_chunk(
            queries[:, c0 : c0 + chunk_width],
            outgoing[..., c0 : c0 + chunk_width],
            state,
            chooser,
            my_slot,
            my_usable,
            device,
            seq_count,
            capacity,
            hold=tuple(states[1:]) if index == 0 else (),
        )
        if index == 0:
            held = piece[3]
        pieces.append(piece)
    query_grads = jnp.concatenate([p[0] for p in pieces], axis=-1)
    totals = jnp.concatenate([p[1] for p in pieces], axis=-1)
    rim_terms = jnp.concatenate([p[2] for p in pieces], axis=-1)
    rim_terms, totals = lax.optimization_barrier((rim_terms, totals))
    widened = extended_2(rim_terms.astype(jnp.bfloat16), (("seq", 1),), BLOCK).astype(
        rim_terms.dtype
    )
    edges = jnp.concatenate(
        [
            widened[:, None, :BLOCK],
            jnp.zeros((2, per_dev - 2, BLOCK, features), widened.dtype),
            widened[:, None, -BLOCK:],
        ],
        axis=1,
    )
    totals = totals + edges
    grad_rows = query_grads.reshape(tokens, features).astype(jnp.bfloat16)
    key_rows = totals[0].reshape(tokens, features).astype(jnp.bfloat16)
    value_rows = totals[1].reshape(tokens, features).astype(jnp.bfloat16)
    result = jnp.stack([grad_rows, key_rows, value_rows])
    result = lax.all_to_all(result, "head", split_axis=1, concat_axis=2, tiled=True)
    return (result[0], result[1], result[2])


def solution(mesh):
    in_specs = (
        P(("seq", "head"), None),
        P(("seq", "head"), None),
        P(("seq", "head"), None),
        P(("seq", "head"), None),
        P(),
    )
    out_specs = (P(("seq", "head"), None), P(("seq", "head"), None), P(("seq", "head"), None))
    return jax.shard_map(
        on_device, mesh=mesh, in_specs=in_specs, out_specs=out_specs, check_vma=False
    )
```

profile of v0, /device:TPU:17, one launch (start us, length us, event | category | flops | bytes accessed | tf_op | source)
XLA Modules:
  0.0 576.9 jit_solution(925645524547696815)
XLA Ops:
  2.0 3.9 copy.856
  5.9 4.1 all-to-all-start
  12.7 3.8 copy.871
  16.7 18.7 %all-to-all-done = bf16[2,160,2048]{1,0,2:T(2,128)(2,1)S(1)} async-done(((bf16[2,160,2048]{1,0,2:T(2,128)(2,1)}), bf16[2,160,2048]{1,0,2:T(2,128)(2,1)S(1)}, u32[]{:S(2)}, u32[]{:S(2)}) %all-to-all-start) | async-done | bytes 1310752 | tf_op jit(solution)/shard_map/all_to_all | solution.py:254
  35.5 4.5 all-to-all-start.1
  39.9 3.7 copy.987
  50.1 4.7 collective-permute-start.14
  62.8 14.1 %collective-permute-done.11 = bf16[2,128,512]{2,1,0:T(8,128)(2,1)S(1)} collective-permute-done((bf16[2,128,512]{2,1,0:T(8,128)(2,1)S(1)}, bf16[2,128,512]{2,1,0:T(8,128)(2,1)S(1)}, u32[]{:S(2)}, u32[]{:S(2)}) %collective-permute-start.11) | collective-permute-done | bytes 262176 | tf_op jit(solution)/shard_map/ppermute | solution.py:23
  84.4 4.5 copy.876
  88.9 9.9 %all-to-all-start.2 = ((bf16[64,2,64,256]{3,2,1,0:T(8,128)(2,1)}), bf16[64,2,64,256]{3,2,1,0:T(8,128)(2,1)}, u32[]{:S(2)}, u32[]{:S(2)}) async-start(bf16[64,2,64,256]{3,2,1,0:T(8,128)(2,1)} %copy.876), calls=%async_computation.2 | async-start | bytes 8388608 | tf_op jit(solution)/shard_map/all_to_all | solution.py:141
  101.8 5.6 copy.986
  122.8 4.5 copy.898
  130.9 61.6 %all-to-all-done.2 = bf16[64,2,64,256]{3,2,1,0:T(8,128)(2,1)} async-done(((bf16[64,2,64,256]{3,2,1,0:T(8,128)(2,1)}), bf16[64,2,64,256]{3,2,1,0:T(8,128)(2,1)}, u32[]{:S(2)}, u32[]{:S(2)}) %all-to-all-start.2) | async-done | bytes 4194336 | tf_op jit(solution)/shard_map/all_to_all | solution.py:141
  192.5 8.4 %all-to-all-start.3 = ((bf16[64,2,64,256]{3,2,1,0:T(8,128)(2,1)}), bf16[64,2,64,256]{3,2,1,0:T(8,128)(2,1)}, u32[]{:S(2)}, u32[]{:S(2)}) async-start(bf16[64,2,64,256]{3,2,1,0:T(8,128)(2,1)} %copy.898), calls=%async_computation.3 | async-start | bytes 8388608 | tf_op jit(solution)/shard_map/all_to_all | solution.py:141
  213.3 4.5 reshape_squeeze.28
  231.5 4.2 gather_fusion.1
  272.3 4.6 copy.935
  276.9 17.7 %all-to-all-done.3 = bf16[64,2,64,256]{3,2,1,0:T(8,128)(2,1)} async-done(((bf16[64,2,64,256]{3,2,1,0:T(8,128)(2,1)}), bf16[64,2,64,256]{3,2,1,0:T(8,128)(2,1)}, u32[]{:S(2)}, u32[]{:S(2)}) %all-to-all-start.3) | async-done | bytes 4194336 | tf_op jit(solution)/shard_map/all_to_all | solution.py:141
  294.6 8.0 %all-to-all-start.4 = ((bf16[64,2,64,256]{3,2,1,0:T(8,128)(2,1)}), bf16[64,2,64,256]{3,2,1,0:T(8,128)(2,1)}, u32[]{:S(2)}, u32[]{:S(2)}) async-start(bf16[64,2,64,256]{3,2,1,0:T(8,128)(2,1)} %copy.935), calls=%async_computation.4 | async-start | bytes 8388608 | tf_op jit(solution)/shard_map/all_to_all | solution.py:208
  312.5 3.5 copy.904
  344.7 4.4 copy.953
  349.0 47.4 %all-to-all-done.4 = bf16[64,2,64,256]{3,2,1,0:T(8,128)(2,1)} async-done(((bf16[64,2,64,256]{3,2,1,0:T(8,128)(2,1)}), bf16[64,2,64,256]{3,2,1,0:T(8,128)(2,1)}, u32[]{:S(2)}, u32[]{:S(2)}) %all-to-all-start.4) | async-done | bytes 4194336 | tf_op jit(solution)/shard_map/all_to_all | solution.py:208
  396.5 8.5 %all-to-all-start.5 = ((bf16[64,2,64,256]{3,2,1,0:T(8,128)(2,1)}), bf16[64,2,64,256]{3,2,1,0:T(8,128)(2,1)}, u32[]{:S(2)}, u32[]{:S(2)}) async-start(bf16[64,2,64,256]{3,2,1,0:T(8,128)(2,1)} %copy.953), calls=%async_computation.5 | async-start | bytes 8388608 | tf_op jit(solution)/shard_map/all_to_all | solution.py:208
  412.0 3.8 reshape.519
  420.4 4.2 reshape.518
  432.8 4.1 reshape.520
  451.2 3.7 convert_reduce_fusion.1
  454.9 43.6 %all-to-all-done.5 = bf16[64,2,64,256]{3,2,1,0:T(8,128)(2,1)} async-done(((bf16[64,2,64,256]{3,2,1,0:T(8,128)(2,1)}), bf16[64,2,64,256]{3,2,1,0:T(8,128)(2,1)}, u32[]{:S(2)}, u32[]{:S(2)}) %all-to-all-start.5) | async-done | bytes 4194336 | tf_op jit(solution)/shard_map/all_to_all | solution.py:208
  502.4 4.7 fusion.1
  508.9 5.4 bitcast_add_fusion
  516.9 5.6 collective-permute-start.18
  535.0 36.4 %all_to_all.65 = bf16[3,640,512]{2,0,1:T(4,128)(2,1)S(1)} all-to-all(bf16[3,640,512]{2,0,1:T(4,128)(2,1)S(1)} %copy.962), channel_id=1, replica_groups=mesh['seq'=64,'head'=4] {'head'}, dimensions={1} | all-to-all | bytes 3932160 | tf_op jit(solution)/shard_map/all_to_all | solution.py:347
  (369 shorter events, 208.0 us)
Async XLA Ops:
  5.9 29.6 %all-to-all-start = ((bf16[2,160,2048]{1,0,2:T(2,128)(2,1)}), bf16[2,160,2048]{1,0,2:T(2,128)(2,1)S(1)}, u32[]{:S(2)}, u32[]{:S(2)}) async-start(bf16[2,160,2048]{1,0,2:T(2,128)(2,1)} %copy.856), calls=%async_computation | async-start | bytes 4194304 | tf_op jit(solution)/shard_map/all_to_all | solution.py:254
  35.5 53.5 %all-to-all-start.1 = ((bf16[2,160,2048]{1,0,2:T(2,128)(2,1)}), bf16[2,160,2048]{1,0,2:T(2,128)(2,1)}, u32[]{:S(2)}, u32[]{:S(2)}) async-start(bf16[2,160,2048]{1,0,2:T(2,128)(2,1)} %copy.871), calls=%async_computation.1 | async-start | bytes 4194304 | tf_op jit(solution)/shard_map/all_to_all | solution.py:257
  44.5 3.8 collective-permute-start
  45.2 3.8 collective-permute-start.1
  46.2 31.4 %copy-start.60 = (bf16[64,10]{0,1:T(8,128)(2,1)}, bf16[64,10]{0,1:T(8,128)(2,1)S(1)}, u32[]{:S(2)}) copy-start(bf16[64,10]{0,1:T(8,128)(2,1)S(1)} %fusion.87) | copy-start | bytes 3844
  46.2 3.9 collective-permute-start.2
  46.9 7.9 %collective-permute-start.3 = (bf16[2,128,512]{2,1,0:T(8,128)(2,1)S(1)}, bf16[2,128,512]{2,1,0:T(8,128)(2,1)S(1)}, u32[]{:S(2)}, u32[]{:S(2)}) collective-permute-start(bf16[2,128,512]{2,1,0:T(8,128)(2,1)S(1)} %maximum_select_fusion), channel_id=1, source_target_pairs={{0,128},{1,129},{2,130},{3,131}} | collective-permute-start | bytes 786440 | tf_op jit(solution)/shard_map/ppermute | solution.py:19
  47.6 9.1 %collective-permute-start.4 = (bf16[2,128,512]{2,1,0:T(8,128)(2,1)S(1)}, bf16[2,128,512]{2,1,0:T(8,128)(2,1)S(1)}, u32[]{:S(2)}, u32[]{:S(2)}) collective-permute-start(bf16[2,128,512]{2,1,0:T(8,128)(2,1)S(1)} %maximum_select_fusion), channel_id=1, source_target_pairs={{0,160},{1,161},{2,162},{3,163}} | collective-permute-start | bytes 786440 | tf_op jit(solution)/shard_map/ppermute | solution.py:19
  48.3 8.4 %collective-permute-start.5 = (bf16[2,128,512]{2,1,0:T(8,128)(2,1)S(1)}, bf16[2,128,512]{2,1,0:T(8,128)(2,1)S(1)}, u32[]{:S(2)}, u32[]{:S(2)}) collective-permute-start(bf16[2,128,512]{2,1,0:T(8,128)(2,1)S(1)} %maximum_select_fusion), channel_id=1, source_target_pairs={{0,192},{1,193},{2,194},{3,195}} | collective-permute-start | bytes 786440 | tf_op jit(solution)/shard_map/ppermute | solution.py:19
  49.0 7.7 %collective-permute-start.6 = (bf16[2,128,512]{2,1,0:T(8,128)(2,1)S(1)}, bf16[2,128,512]{2,1,0:T(8,128)(2,1)S(1)}, u32[]{:S(2)}, u32[]{:S(2)}) collective-permute-start(bf16[2,128,512]{2,1,0:T(8,128)(2,1)S(1)} %maximum_select_fusion), channel_id=1, source_target_pairs={{0,224},{1,225},{2,226},{3,227}} | collective-permute-start | bytes 786440 | tf_op jit(solution)/shard_map/ppermute | solution.py:19
  50.1 9.9 %collective-permute-start.14 = (bf16[2,64,512]{2,1,0:T(8,128)(2,1)S(1)}, bf16[2,64,512]{2,1,0:T(8,128)(2,1)S(1)}, u32[]{:S(2)}, u32[]{:S(2)}) collective-permute-start(bf16[2,64,512]{2,1,0:T(8,128)(2,1)S(1)} %get-tuple-element.75), channel_id=1, source_target_pairs={{0,4},{4,8},{8,12},{12,16},{16,20},{20,24},{24,28},{28,32},{32,36}... | collective-permute-start | bytes 393224 | tf_op jit(solution)/shard_map/ppermute | solution.py:61
  54.8 6.7 %collective-permute-start.15 = (bf16[2,64,512]{2,1,0:T(8,128)(2,1)S(1)}, bf16[2,64,512]{2,1,0:T(8,128)(2,1)S(1)}, u32[]{:S(2)}, u32[]{:S(2)}) collective-permute-start(bf16[2,64,512]{2,1,0:T(8,128)(2,1)S(1)} %get-tuple-element.76), channel_id=1, source_target_pairs={{4,0},{8,4},{12,8},{16,12},{20,16},{24,20},{28,24},{32,28},{36,32}... | collective-permute-start | bytes 393224 | tf_op jit(solution)/shard_map/ppermute | solution.py:62
  56.9 5.2 collective-permute-start.10
  57.6 19.3 %collective-permute-start.11 = (bf16[2,128,512]{2,1,0:T(8,128)(2,1)S(1)}, bf16[2,128,512]{2,1,0:T(8,128)(2,1)S(1)}, u32[]{:S(2)}, u32[]{:S(2)}) collective-permute-start(bf16[2,128,512]{2,1,0:T(8,128)(2,1)S(1)} %add_add_fusion.1), channel_id=1, source_target_pairs={{0,20},{32,52},{64,84},{96,116},{128,148},{160,180},{192,212},{224... | collective-permute-start | bytes 786440 | tf_op jit(solution)/shard_map/ppermute | solution.py:23
  59.3 21.9 %collective-permute-start.12 = (bf16[2,128,512]{2,1,0:T(8,128)(2,1)S(1)}, bf16[2,128,512]{2,1,0:T(8,128)(2,1)S(1)}, u32[]{:S(2)}, u32[]{:S(2)}) collective-permute-start(bf16[2,128,512]{2,1,0:T(8,128)(2,1)S(1)} %add_add_fusion.1), channel_id=1, source_target_pairs={{0,24},{32,56},{64,88},{96,120},{128,152},{160,184},{192,216},{224... | collective-permute-start | bytes 786440 | tf_op jit(solution)/shard_map/ppermute | solution.py:23
  60.0 21.2 %collective-permute-start.13 = (bf16[2,128,512]{2,1,0:T(8,128)(2,1)S(1)}, bf16[2,128,512]{2,1,0:T(8,128)(2,1)S(1)}, u32[]{:S(2)}, u32[]{:S(2)}) collective-permute-start(bf16[2,128,512]{2,1,0:T(8,128)(2,1)S(1)} %add_add_fusion.1), channel_id=1, source_target_pairs={{0,28},{32,60},{64,92},{96,124},{128,156},{160,188},{192,220},{224... | collective-permute-start | bytes 786440 | tf_op jit(solution)/shard_map/ppermute | solution.py:23
  61.4 19.8 %collective-permute-start.7 = (bf16[2,128,512]{2,1,0:T(8,128)(2,1)S(1)}, bf16[2,128,512]{2,1,0:T(8,128)(2,1)S(1)}, u32[]{:S(2)}, u32[]{:S(2)}) collective-permute-start(bf16[2,128,512]{2,1,0:T(8,128)(2,1)S(1)} %add_add_fusion.1), channel_id=1, source_target_pairs={{0,4},{32,36},{64,68},{96,100},{128,132},{160,164},{192,196},{224,... | collective-permute-start | bytes 786440 | tf_op jit(solution)/shard_map/ppermute | solution.py:23
  62.1 19.1 %collective-permute-start.8 = (bf16[2,128,512]{2,1,0:T(8,128)(2,1)S(1)}, bf16[2,128,512]{2,1,0:T(8,128)(2,1)S(1)}, u32[]{:S(2)}, u32[]{:S(2)}) collective-permute-start(bf16[2,128,512]{2,1,0:T(8,128)(2,1)S(1)} %add_add_fusion.1), channel_id=1, source_target_pairs={{0,8},{32,40},{64,72},{96,104},{128,136},{160,168},{192,200},{224,... | collective-permute-start | bytes 786440 | tf_op jit(solution)/shard_map/ppermute | solution.py:23
  76.9 4.3 collective-permute-start.9
  88.9 103.6 %all-to-all-start.2 = ((bf16[64,2,64,256]{3,2,1,0:T(8,128)(2,1)}), bf16[64,2,64,256]{3,2,1,0:T(8,128)(2,1)}, u32[]{:S(2)}, u32[]{:S(2)}) async-start(bf16[64,2,64,256]{3,2,1,0:T(8,128)(2,1)} %copy.876), calls=%async_computation.2 | async-start | bytes 8388608 | tf_op jit(solution)/shard_map/all_to_all | solution.py:141
  192.5 102.1 %all-to-all-start.3 = ((bf16[64,2,64,256]{3,2,1,0:T(8,128)(2,1)}), bf16[64,2,64,256]{3,2,1,0:T(8,128)(2,1)}, u32[]{:S(2)}, u32[]{:S(2)}) async-start(bf16[64,2,64,256]{3,2,1,0:T(8,128)(2,1)} %copy.898), calls=%async_computation.3 | async-start | bytes 8388608 | tf_op jit(solution)/shard_map/all_to_all | solution.py:141
  206.3 5.2 copy-start.3
  211.5 6.2 %copy-start.5 = (bf16[10,5,64,2,128]{4,3,2,1,0:T(2,128)(2,1)}, bf16[10,5,64,2,128]{4,3,2,1,0:T(2,128)(2,1)S(1)}, u32[]{:S(2)}) copy-start(bf16[10,5,64,2,128]{4,3,2,1,0:T(2,128)(2,1)S(1)} %reshape_squeeze.27) | copy-start | bytes 4915204
  258.1 10.4 %collective-permute-start.16 = (f32[2,64,256]{2,1,0:T(8,128)}, f32[2,64,256]{2,1,0:T(8,128)}, u32[]{:S(2)}, u32[]{:S(2)}) collective-permute-start(f32[2,64,256]{2,1,0:T(8,128)} %bitcast.346), channel_id=1, source_target_pairs={{0,4},{4,0},{8,12},{12,8},{16,20},{20,16},{24,28},{28,24},{32,36},... | collective-permute-start | bytes 393224 | tf_op jit(solution)/shard_map/ppermute | solution.py:200
  294.6 101.9 %all-to-all-start.4 = ((bf16[64,2,64,256]{3,2,1,0:T(8,128)(2,1)}), bf16[64,2,64,256]{3,2,1,0:T(8,128)(2,1)}, u32[]{:S(2)}, u32[]{:S(2)}) async-start(bf16[64,2,64,256]{3,2,1,0:T(8,128)(2,1)} %copy.935), calls=%async_computation.4 | async-start | bytes 8388608 | tf_op jit(solution)/shard_map/all_to_all | solution.py:208
  324.7 17.1 %collective-permute-start.17 = (f32[2,64,256]{2,1,0:T(8,128)S(1)}, f32[2,64,256]{2,1,0:T(8,128)S(1)}, u32[]{:S(2)}, u32[]{:S(2)}) collective-permute-start(f32[2,64,256]{2,1,0:T(8,128)S(1)} %bitcast.423), channel_id=1, source_target_pairs={{0,4},{4,0},{8,12},{12,8},{16,20},{20,16},{24,28},{28,24},{32,36},... | collective-permute-start | bytes 393224 | tf_op jit(solution)/shard_map/ppermute | solution.py:200
  396.5 102.1 %all-to-all-start.5 = ((bf16[64,2,64,256]{3,2,1,0:T(8,128)(2,1)}), bf16[64,2,64,256]{3,2,1,0:T(8,128)(2,1)}, u32[]{:S(2)}, u32[]{:S(2)}) async-start(bf16[64,2,64,256]{3,2,1,0:T(8,128)(2,1)} %copy.953), calls=%async_computation.5 | async-start | bytes 8388608 | tf_op jit(solution)/shard_map/all_to_all | solution.py:208
  514.3 10.0 %copy-start.24 = (bf16[10,2,64,3,64]{2,4,3,1,0:T(8,128)(2,1)S(1)}, bf16[10,2,64,3,64]{2,4,3,1,0:T(8,128)(2,1)}, u32[]{:S(2)}) copy-start(bf16[10,2,64,3,64]{2,4,3,1,0:T(8,128)(2,1)} %copy-done.23) | copy-start | bytes 1474564
  514.3 10.0 %copy-start.27 = (bf16[10,3,64,2,128]{4,3,2,1,0:T(2,128)(2,1)S(1)}, bf16[10,3,64,2,128]{4,3,2,1,0:T(2,128)(2,1)}, u32[]{:S(2)}) copy-start(bf16[10,3,64,2,128]{4,3,2,1,0:T(2,128)(2,1)} %copy-done.26) | copy-start | bytes 2949124
  516.9 8.0 %copy-start.57 = (bf16[10,64,2,128]{3,1,2,0:T(8,128)(2,1)S(1)}, bf16[10,64,2,128]{3,1,2,0:T(8,128)(2,1)}, u32[]{:S(2)}) copy-start(bf16[10,64,2,128]{3,1,2,0:T(8,128)(2,1)} %fusion.38) | copy-start | bytes 983044
  516.9 9.2 %collective-permute-start.18 = (bf16[2,64,512]{2,1,0:T(8,128)(2,1)S(1)}, bf16[2,64,512]{2,1,0:T(8,128)(2,1)S(1)}, u32[]{:S(2)}, u32[]{:S(2)}) collective-permute-start(bf16[2,64,512]{2,1,0:T(8,128)(2,1)S(1)} %get-tuple-element.89), channel_id=1, source_target_pairs={{0,4},{4,8},{8,12},{12,16},{16,20},{20,24},{24,28},{28,32},{32,36}... | collective-permute-start | bytes 393224 | tf_op jit(solution)/shard_map/ppermute | solution.py:61
  522.4 6.3 %collective-permute-start.19 = (bf16[2,64,512]{2,1,0:T(8,128)(2,1)S(1)}, bf16[2,64,512]{2,1,0:T(8,128)(2,1)S(1)}, u32[]{:S(2)}, u32[]{:S(2)}) collective-permute-start(bf16[2,64,512]{2,1,0:T(8,128)(2,1)S(1)} %get-tuple-element.90), channel_id=1, source_target_pairs={{4,0},{8,4},{12,8},{16,12},{20,16},{24,20},{28,24},{32,28},{36,32}... | collective-permute-start | bytes 393224 | tf_op jit(solution)/shard_map/ppermute | solution.py:62
  (59 other events, 134.5 us)
where the time goes:
time: 588 us; the launch traced here: 577 us
  waiting for transfers between devices  207 us (35%)
  local copies, waits for them, and re-layouts  184 us (31%)
  starting transfers between devices  68.9 us (12%)
  other arithmetic  44.6 us (8%)
  blocking collectives  36.4 us (6%)
  matrix products  33.4 us (6%)
    all_to_all x2, waiting for transfers between devices, attend_chunk(): lax.all_to_all(outgoing_back, 'seq', split_axis=0, concat_axis=0, tiled=T...  91.1 us
    all_to_all x2, waiting for transfers between devices, attend_chunk(): lax.all_to_all(outgoing, 'seq', split_axis=0, concat_axis=0, tiled=True)  79.3 us
    all_to_all x1, blocking collectives, on_device(): lax.all_to_all(result, 'head', split_axis=1, concat_axis=2, tiled=True)  36.4 us
    another operation x10, local copies, waits for them, and re-layouts, attend_chunk(): jnp.stack([key_terms, value_terms]).reshape(2, per_dev, 3, BLOCK, features)  25.3 us
    unnamed x137, local copies, waits for them, and re-layouts  24.6 us
    all_to_all x1, waiting for transfers between devices, on_device(): lax.all_to_all(kv_stacked, 'head', split_axis=2, concat_axis=1, tiled=True)  18.7 us
    all_to_all x2, starting transfers between devices, attend_chunk(): lax.all_to_all(outgoing, 'seq', split_axis=0, concat_axis=0, tiled=True)  18.3 us
    all_to_all x2, starting transfers between devices, attend_chunk(): lax.all_to_all(outgoing_back, 'seq', split_axis=0, concat_axis=0, tiled=T...  16.5 us
  transfers between devices with their start and end apart: 26, of which 8 were waited for; matrix products, arithmetic and copies ran while one was open for 36% of the time, Pallas kernels for 0%

commit v1 on v0

--- a/solution.py
+++ b/solution.py
@@ -344,7 +344,10 @@
     key_rows = totals[0].reshape(tokens, features).astype(jnp.bfloat16)
     value_rows = totals[1].reshape(tokens, features).astype(jnp.bfloat16)
     result = jnp.stack([grad_rows, key_rows, value_rows])
-    result = lax.all_to_all(result, "head", split_axis=1, concat_axis=2, tiled=True)
+    result = jnp.concatenate(
+        lax.all_to_all(jnp.stack(jnp.split(result, lax.axis_size("head"), axis=1)), "head", 0, 0),
+        axis=2,
+    )
     return (result[0], result[1], result[2])
 
 

time: 588 us -> 579 us (0.985)
  blocking collectives: 36.4 us -> 29.4 us
    all_to_all x1, blocking collectives: 36.4 us -> 29.4 us  [on_device(): lax.all_to_all(jnp.stack(jnp.split(result, lax.axis_size('head'), axis=1)...]
where the time goes in v1:
time: 579 us; the launch traced here: 568 us
  waiting for transfers between devices  207 us (36%)
  local copies, waits for them, and re-layouts  182 us (31%)
  starting transfers between devices  68.9 us (12%)
  other arithmetic  44.9 us (8%)
  matrix products  33.4 us (6%)
  blocking collectives  29.4 us (5%)
    all_to_all x2, waiting for transfers between devices, attend_chunk(): lax.all_to_all(outgoing_back, 'seq', split_axis=0, concat_axis=0, tiled=T...  91 us
    all_to_all x2, waiting for transfers between devices, attend_chunk(): lax.all_to_all(outgoing, 'seq', split_axis=0, concat_axis=0, tiled=True)  79.3 us
    all_to_all x1, blocking collectives, on_device(): lax.all_to_all(jnp.stack(jnp.split(result, lax.axis_size('head'), axis=1)...  29.4 us
    another operation x10, local copies, waits for them, and re-layouts, attend_chunk(): jnp.stack([key_terms, value_terms]).reshape(2, per_dev, 3, BLOCK, features)  25.3 us
    unnamed x137, local copies, waits for them, and re-layouts  24.6 us
    all_to_all x1, waiting for transfers between devices, on_device(): lax.all_to_all(kv_stacked, 'head', split_axis=2, concat_axis=1, tiled=True)  18.8 us
    all_to_all x2, starting transfers between devices, attend_chunk(): lax.all_to_all(outgoing, 'seq', split_axis=0, concat_axis=0, tiled=True)  18.3 us
    all_to_all x2, starting transfers between devices, attend_chunk(): lax.all_to_all(outgoing_back, 'seq', split_axis=0, concat_axis=0, tiled=T...  16.5 us
  transfers between devices with their start and end apart: 26, of which 8 were waited for; matrix products, arithmetic and copies ran while one was open for 36% of the time, Pallas kernels for 0%

profile of v1, /device:TPU:17, one launch (start us, length us, event | category | flops | bytes accessed | tf_op | source)
XLA Modules:
  0.0 567.9 jit_solution(13782472725591542058)
XLA Ops:
  2.0 3.8 copy.853
  5.9 4.1 all-to-all-start
  12.6 3.8 copy.868
  16.7 18.8 %all-to-all-done = bf16[2,160,2048]{1,0,2:T(2,128)(2,1)S(1)} async-done(((bf16[2,160,2048]{1,0,2:T(2,128)(2,1)}), bf16[2,160,2048]{1,0,2:T(2,128)(2,1)S(1)}, u32[]{:S(2)}, u32[]{:S(2)}) %all-to-all-start) | async-done | bytes 1310752 | tf_op jit(solution)/shard_map/all_to_all | solution.py:254
  35.4 4.5 all-to-all-start.1
  39.9 3.7 copy.982
  50.0 4.7 collective-permute-start.14
  62.8 14.1 %collective-permute-done.11 = bf16[2,128,512]{2,1,0:T(8,128)(2,1)S(1)} collective-permute-done((bf16[2,128,512]{2,1,0:T(8,128)(2,1)S(1)}, bf16[2,128,512]{2,1,0:T(8,128)(2,1)S(1)}, u32[]{:S(2)}, u32[]{:S(2)}) %collective-permute-start.11) | collective-permute-done | bytes 262176 | tf_op jit(solution)/shard_map/ppermute | solution.py:23
  84.4 4.5 copy.873
  88.9 9.9 %all-to-all-start.2 = ((bf16[64,2,64,256]{3,2,1,0:T(8,128)(2,1)}), bf16[64,2,64,256]{3,2,1,0:T(8,128)(2,1)}, u32[]{:S(2)}, u32[]{:S(2)}) async-start(bf16[64,2,64,256]{3,2,1,0:T(8,128)(2,1)} %copy.873), calls=%async_computation.2 | async-start | bytes 8388608 | tf_op jit(solution)/shard_map/all_to_all | solution.py:141
  101.8 5.6 copy.981
  122.8 4.5 copy.895
  130.9 61.6 %all-to-all-done.2 = bf16[64,2,64,256]{3,2,1,0:T(8,128)(2,1)} async-done(((bf16[64,2,64,256]{3,2,1,0:T(8,128)(2,1)}), bf16[64,2,64,256]{3,2,1,0:T(8,128)(2,1)}, u32[]{:S(2)}, u32[]{:S(2)}) %all-to-all-start.2) | async-done | bytes 4194336 | tf_op jit(solution)/shard_map/all_to_all | solution.py:141
  192.4 8.4 %all-to-all-start.3 = ((bf16[64,2,64,256]{3,2,1,0:T(8,128)(2,1)}), bf16[64,2,64,256]{3,2,1,0:T(8,128)(2,1)}, u32[]{:S(2)}, u32[]{:S(2)}) async-start(bf16[64,2,64,256]{3,2,1,0:T(8,128)(2,1)} %copy.895), calls=%async_computation.3 | async-start | bytes 8388608 | tf_op jit(solution)/shard_map/all_to_all | solution.py:141
  213.2 4.4 reshape_squeeze.28
  231.5 4.2 gather_fusion.1
  272.2 4.6 copy.932
  276.8 17.7 %all-to-all-done.3 = bf16[64,2,64,256]{3,2,1,0:T(8,128)(2,1)} async-done(((bf16[64,2,64,256]{3,2,1,0:T(8,128)(2,1)}), bf16[64,2,64,256]{3,2,1,0:T(8,128)(2,1)}, u32[]{:S(2)}, u32[]{:S(2)}) %all-to-all-start.3) | async-done | bytes 4194336 | tf_op jit(solution)/shard_map/all_to_all | solution.py:141
  294.5 8.0 %all-to-all-start.4 = ((bf16[64,2,64,256]{3,2,1,0:T(8,128)(2,1)}), bf16[64,2,64,256]{3,2,1,0:T(8,128)(2,1)}, u32[]{:S(2)}, u32[]{:S(2)}) async-start(bf16[64,2,64,256]{3,2,1,0:T(8,128)(2,1)} %copy.932), calls=%async_computation.4 | async-start | bytes 8388608 | tf_op jit(solution)/shard_map/all_to_all | solution.py:208
  312.4 3.5 copy.901
  344.6 4.4 copy.950
  349.0 47.4 %all-to-all-done.4 = bf16[64,2,64,256]{3,2,1,0:T(8,128)(2,1)} async-done(((bf16[64,2,64,256]{3,2,1,0:T(8,128)(2,1)}), bf16[64,2,64,256]{3,2,1,0:T(8,128)(2,1)}, u32[]{:S(2)}, u32[]{:S(2)}) %all-to-all-start.4) | async-done | bytes 4194336 | tf_op jit(solution)/shard_map/all_to_all | solution.py:208
  396.4 8.4 %all-to-all-start.5 = ((bf16[64,2,64,256]{3,2,1,0:T(8,128)(2,1)}), bf16[64,2,64,256]{3,2,1,0:T(8,128)(2,1)}, u32[]{:S(2)}, u32[]{:S(2)}) async-start(bf16[64,2,64,256]{3,2,1,0:T(8,128)(2,1)} %copy.950), calls=%async_computation.5 | async-start | bytes 8388608 | tf_op jit(solution)/shard_map/all_to_all | solution.py:208
  412.0 3.8 reshape.524
  420.4 4.1 reshape.523
  432.7 4.1 reshape.525
  451.2 3.7 convert_reduce_fusion.1
  454.9 43.6 %all-to-all-done.5 = bf16[64,2,64,256]{3,2,1,0:T(8,128)(2,1)} async-done(((bf16[64,2,64,256]{3,2,1,0:T(8,128)(2,1)}), bf16[64,2,64,256]{3,2,1,0:T(8,128)(2,1)}, u32[]{:S(2)}, u32[]{:S(2)}) %all-to-all-start.5) | async-done | bytes 4194336 | tf_op jit(solution)/shard_map/all_to_all | solution.py:208
  502.3 4.7 fusion.1
  508.9 5.4 bitcast_add_fusion
  516.8 5.6 collective-permute-start.18
  533.7 29.4 %all_to_all.55 = bf16[4,3,160,512]{3,2,1,0:T(8,128)(2,1)S(1)} all-to-all(bf16[4,3,160,512]{3,2,1,0:T(8,128)(2,1)S(1)} %pad_maximum_fusion.6), channel_id=1, replica_groups=mesh['seq'=64,'head'=4] {'head'}, dimensions={0} | all-to-all | bytes 3932160 | tf_op jit(solution)/shard_map/all_to_all | solution.py:348
  (369 shorter events, 206.2 us)
Async XLA Ops:
  5.9 29.6 %all-to-all-start = ((bf16[2,160,2048]{1,0,2:T(2,128)(2,1)}), bf16[2,160,2048]{1,0,2:T(2,128)(2,1)S(1)}, u32[]{:S(2)}, u32[]{:S(2)}) async-start(bf16[2,160,2048]{1,0,2:T(2,128)(2,1)} %copy.853), calls=%async_computation | async-start | bytes 4194304 | tf_op jit(solution)/shard_map/all_to_all | solution.py:254
  35.4 53.5 %all-to-all-start.1 = ((bf16[2,160,2048]{1,0,2:T(2,128)(2,1)}), bf16[2,160,2048]{1,0,2:T(2,128)(2,1)}, u32[]{:S(2)}, u32[]{:S(2)}) async-start(bf16[2,160,2048]{1,0,2:T(2,128)(2,1)} %copy.868), calls=%async_computation.1 | async-start | bytes 4194304 | tf_op jit(solution)/shard_map/all_to_all | solution.py:257
  44.4 3.8 collective-permute-start
  45.1 3.8 collective-permute-start.1
  46.1 31.4 %copy-start.60 = (bf16[64,10]{0,1:T(8,128)(2,1)}, bf16[64,10]{0,1:T(8,128)(2,1)S(1)}, u32[]{:S(2)}) copy-start(bf16[64,10]{0,1:T(8,128)(2,1)S(1)} %fusion.87) | copy-start | bytes 3844
  46.1 3.9 collective-permute-start.2
  46.8 7.9 %collective-permute-start.3 = (bf16[2,128,512]{2,1,0:T(8,128)(2,1)S(1)}, bf16[2,128,512]{2,1,0:T(8,128)(2,1)S(1)}, u32[]{:S(2)}, u32[]{:S(2)}) collective-permute-start(bf16[2,128,512]{2,1,0:T(8,128)(2,1)S(1)} %maximum_select_fusion), channel_id=1, source_target_pairs={{0,128},{1,129},{2,130},{3,131}} | collective-permute-start | bytes 786440 | tf_op jit(solution)/shard_map/ppermute | solution.py:19
  47.5 9.1 %collective-permute-start.4 = (bf16[2,128,512]{2,1,0:T(8,128)(2,1)S(1)}, bf16[2,128,512]{2,1,0:T(8,128)(2,1)S(1)}, u32[]{:S(2)}, u32[]{:S(2)}) collective-permute-start(bf16[2,128,512]{2,1,0:T(8,128)(2,1)S(1)} %maximum_select_fusion), channel_id=1, source_target_pairs={{0,160},{1,161},{2,162},{3,163}} | collective-permute-start | bytes 786440 | tf_op jit(solution)/shard_map/ppermute | solution.py:19
  48.2 8.4 %collective-permute-start.5 = (bf16[2,128,512]{2,1,0:T(8,128)(2,1)S(1)}, bf16[2,128,512]{2,1,0:T(8,128)(2,1)S(1)}, u32[]{:S(2)}, u32[]{:S(2)}) collective-permute-start(bf16[2,128,512]{2,1,0:T(8,128)(2,1)S(1)} %maximum_select_fusion), channel_id=1, source_target_pairs={{0,192},{1,193},{2,194},{3,195}} | collective-permute-start | bytes 786440 | tf_op jit(solution)/shard_map/ppermute | solution.py:19
  48.9 7.7 %collective-permute-start.6 = (bf16[2,128,512]{2,1,0:T(8,128)(2,1)S(1)}, bf16[2,128,512]{2,1,0:T(8,128)(2,1)S(1)}, u32[]{:S(2)}, u32[]{:S(2)}) collective-permute-start(bf16[2,128,512]{2,1,0:T(8,128)(2,1)S(1)} %maximum_select_fusion), channel_id=1, source_target_pairs={{0,224},{1,225},{2,226},{3,227}} | collective-permute-start | bytes 786440 | tf_op jit(solution)/shard_map/ppermute | solution.py:19
  50.0 9.9 %collective-permute-start.14 = (bf16[2,64,512]{2,1,0:T(8,128)(2,1)S(1)}, bf16[2,64,512]{2,1,0:T(8,128)(2,1)S(1)}, u32[]{:S(2)}, u32[]{:S(2)}) collective-permute-start(bf16[2,64,512]{2,1,0:T(8,128)(2,1)S(1)} %get-tuple-element.79), channel_id=1, source_target_pairs={{0,4},{4,8},{8,12},{12,16},{16,20},{20,24},{24,28},{28,32},{32,36}... | collective-permute-start | bytes 393224 | tf_op jit(solution)/shard_map/ppermute | solution.py:61
  54.7 6.7 %collective-permute-start.15 = (bf16[2,64,512]{2,1,0:T(8,128)(2,1)S(1)}, bf16[2,64,512]{2,1,0:T(8,128)(2,1)S(1)}, u32[]{:S(2)}, u32[]{:S(2)}) collective-permute-start(bf16[2,64,512]{2,1,0:T(8,128)(2,1)S(1)} %get-tuple-element.80), channel_id=1, source_target_pairs={{4,0},{8,4},{12,8},{16,12},{20,16},{24,20},{28,24},{32,28},{36,32}... | collective-permute-start | bytes 393224 | tf_op jit(solution)/shard_map/ppermute | solution.py:62
  56.8 5.2 collective-permute-start.10
  57.5 19.3 %collective-permute-start.11 = (bf16[2,128,512]{2,1,0:T(8,128)(2,1)S(1)}, bf16[2,128,512]{2,1,0:T(8,128)(2,1)S(1)}, u32[]{:S(2)}, u32[]{:S(2)}) collective-permute-start(bf16[2,128,512]{2,1,0:T(8,128)(2,1)S(1)} %add_add_fusion.1), channel_id=1, source_target_pairs={{0,20},{32,52},{64,84},{96,116},{128,148},{160,180},{192,212},{224... | collective-permute-start | bytes 786440 | tf_op jit(solution)/shard_map/ppermute | solution.py:23
  59.2 21.9 %collective-permute-start.12 = (bf16[2,128,512]{2,1,0:T(8,128)(2,1)S(1)}, bf16[2,128,512]{2,1,0:T(8,128)(2,1)S(1)}, u32[]{:S(2)}, u32[]{:S(2)}) collective-permute-start(bf16[2,128,512]{2,1,0:T(8,128)(2,1)S(1)} %add_add_fusion.1), channel_id=1, source_target_pairs={{0,24},{32,56},{64,88},{96,120},{128,152},{160,184},{192,216},{224... | collective-permute-start | bytes 786440 | tf_op jit(solution)/shard_map/ppermute | solution.py:23
  59.9 21.2 %collective-permute-start.13 = (bf16[2,128,512]{2,1,0:T(8,128)(2,1)S(1)}, bf16[2,128,512]{2,1,0:T(8,128)(2,1)S(1)}, u32[]{:S(2)}, u32[]{:S(2)}) collective-permute-start(bf16[2,128,512]{2,1,0:T(8,128)(2,1)S(1)} %add_add_fusion.1), channel_id=1, source_target_pairs={{0,28},{32,60},{64,92},{96,124},{128,156},{160,188},{192,220},{224... | collective-permute-start | bytes 786440 | tf_op jit(solution)/shard_map/ppermute | solution.py:23
  61.4 19.8 %collective-permute-start.7 = (bf16[2,128,512]{2,1,0:T(8,128)(2,1)S(1)}, bf16[2,128,512]{2,1,0:T(8,128)(2,1)S(1)}, u32[]{:S(2)}, u32[]{:S(2)}) collective-permute-start(bf16[2,128,512]{2,1,0:T(8,128)(2,1)S(1)} %add_add_fusion.1), channel_id=1, source_target_pairs={{0,4},{32,36},{64,68},{96,100},{128,132},{160,164},{192,196},{224,... | collective-permute-start | bytes 786440 | tf_op jit(solution)/shard_map/ppermute | solution.py:23
  62.1 19.1 %collective-permute-start.8 = (bf16[2,128,512]{2,1,0:T(8,128)(2,1)S(1)}, bf16[2,128,512]{2,1,0:T(8,128)(2,1)S(1)}, u32[]{:S(2)}, u32[]{:S(2)}) collective-permute-start(bf16[2,128,512]{2,1,0:T(8,128)(2,1)S(1)} %add_add_fusion.1), channel_id=1, source_target_pairs={{0,8},{32,40},{64,72},{96,104},{128,136},{160,168},{192,200},{224,... | collective-permute-start | bytes 786440 | tf_op jit(solution)/shard_map/ppermute | solution.py:23
  76.8 4.3 collective-permute-start.9
  88.9 103.6 %all-to-all-start.2 = ((bf16[64,2,64,256]{3,2,1,0:T(8,128)(2,1)}), bf16[64,2,64,256]{3,2,1,0:T(8,128)(2,1)}, u32[]{:S(2)}, u32[]{:S(2)}) async-start(bf16[64,2,64,256]{3,2,1,0:T(8,128)(2,1)} %copy.873), calls=%async_computation.2 | async-start | bytes 8388608 | tf_op jit(solution)/shard_map/all_to_all | solution.py:141
  192.4 102.0 %all-to-all-start.3 = ((bf16[64,2,64,256]{3,2,1,0:T(8,128)(2,1)}), bf16[64,2,64,256]{3,2,1,0:T(8,128)(2,1)}, u32[]{:S(2)}, u32[]{:S(2)}) async-start(bf16[64,2,64,256]{3,2,1,0:T(8,128)(2,1)} %copy.895), calls=%async_computation.3 | async-start | bytes 8388608 | tf_op jit(solution)/shard_map/all_to_all | solution.py:141
  206.2 5.2 copy-start.3
  211.4 6.2 %copy-start.5 = (bf16[10,5,64,2,128]{4,3,2,1,0:T(2,128)(2,1)}, bf16[10,5,64,2,128]{4,3,2,1,0:T(2,128)(2,1)S(1)}, u32[]{:S(2)}) copy-start(bf16[10,5,64,2,128]{4,3,2,1,0:T(2,128)(2,1)S(1)} %reshape_squeeze.27) | copy-start | bytes 4915204
  258.1 10.4 %collective-permute-start.16 = (f32[2,64,256]{2,1,0:T(8,128)}, f32[2,64,256]{2,1,0:T(8,128)}, u32[]{:S(2)}, u32[]{:S(2)}) collective-permute-start(f32[2,64,256]{2,1,0:T(8,128)} %bitcast.352), channel_id=1, source_target_pairs={{0,4},{4,0},{8,12},{12,8},{16,20},{20,16},{24,28},{28,24},{32,36},... | collective-permute-start | bytes 393224 | tf_op jit(solution)/shard_map/ppermute | solution.py:200
  294.5 101.9 %all-to-all-start.4 = ((bf16[64,2,64,256]{3,2,1,0:T(8,128)(2,1)}), bf16[64,2,64,256]{3,2,1,0:T(8,128)(2,1)}, u32[]{:S(2)}, u32[]{:S(2)}) async-start(bf16[64,2,64,256]{3,2,1,0:T(8,128)(2,1)} %copy.932), calls=%async_computation.4 | async-start | bytes 8388608 | tf_op jit(solution)/shard_map/all_to_all | solution.py:208
  324.6 17.1 %collective-permute-start.17 = (f32[2,64,256]{2,1,0:T(8,128)S(1)}, f32[2,64,256]{2,1,0:T(8,128)S(1)}, u32[]{:S(2)}, u32[]{:S(2)}) collective-permute-start(f32[2,64,256]{2,1,0:T(8,128)S(1)} %bitcast.429), channel_id=1, source_target_pairs={{0,4},{4,0},{8,12},{12,8},{16,20},{20,16},{24,28},{28,24},{32,36},... | collective-permute-start | bytes 393224 | tf_op jit(solution)/shard_map/ppermute | solution.py:200
  396.4 102.1 %all-to-all-start.5 = ((bf16[64,2,64,256]{3,2,1,0:T(8,128)(2,1)}), bf16[64,2,64,256]{3,2,1,0:T(8,128)(2,1)}, u32[]{:S(2)}, u32[]{:S(2)}) async-start(bf16[64,2,64,256]{3,2,1,0:T(8,128)(2,1)} %copy.950), calls=%async_computation.5 | async-start | bytes 8388608 | tf_op jit(solution)/shard_map/all_to_all | solution.py:208
  514.3 10.0 %copy-start.24 = (bf16[10,2,64,3,64]{2,4,3,1,0:T(8,128)(2,1)S(1)}, bf16[10,2,64,3,64]{2,4,3,1,0:T(8,128)(2,1)}, u32[]{:S(2)}) copy-start(bf16[10,2,64,3,64]{2,4,3,1,0:T(8,128)(2,1)} %copy-done.23) | copy-start | bytes 1474564
  514.3 10.0 %copy-start.27 = (bf16[10,3,64,2,128]{4,3,2,1,0:T(2,128)(2,1)S(1)}, bf16[10,3,64,2,128]{4,3,2,1,0:T(2,128)(2,1)}, u32[]{:S(2)}) copy-start(bf16[10,3,64,2,128]{4,3,2,1,0:T(2,128)(2,1)} %copy-done.26) | copy-start | bytes 2949124
  516.8 8.0 %copy-start.57 = (bf16[10,64,2,128]{3,1,2,0:T(8,128)(2,1)S(1)}, bf16[10,64,2,128]{3,1,2,0:T(8,128)(2,1)}, u32[]{:S(2)}) copy-start(bf16[10,64,2,128]{3,1,2,0:T(8,128)(2,1)} %fusion.38) | copy-start | bytes 983044
  516.8 9.2 %collective-permute-start.18 = (bf16[2,64,512]{2,1,0:T(8,128)(2,1)S(1)}, bf16[2,64,512]{2,1,0:T(8,128)(2,1)S(1)}, u32[]{:S(2)}, u32[]{:S(2)}) collective-permute-start(bf16[2,64,512]{2,1,0:T(8,128)(2,1)S(1)} %get-tuple-element.93), channel_id=1, source_target_pairs={{0,4},{4,8},{8,12},{12,16},{16,20},{20,24},{24,28},{28,32},{32,36}... | collective-permute-start | bytes 393224 | tf_op jit(solution)/shard_map/ppermute | solution.py:61
  522.4 6.3 %collective-permute-start.19 = (bf16[2,64,512]{2,1,0:T(8,128)(2,1)S(1)}, bf16[2,64,512]{2,1,0:T(8,128)(2,1)S(1)}, u32[]{:S(2)}, u32[]{:S(2)}) collective-permute-start(bf16[2,64,512]{2,1,0:T(8,128)(2,1)S(1)} %get-tuple-element.94), channel_id=1, source_target_pairs={{4,0},{8,4},{12,8},{16,12},{20,16},{24,20},{28,24},{32,28},{36,32}... | collective-permute-start | bytes 393224 | tf_op jit(solution)/shard_map/ppermute | solution.py:62
  (59 other events, 134.5 us)
